TPU v7x, 256 devices: a whole 4x4x8 slice. The times are simulated.
256 devices in a mesh: row: 16 (over z, y_hi), col: 16 (over x, y_lo, core).
Axes of the slice: x: 4, y: 4 (y_hi: 2, y_lo: 2; y = y_hi * 2 + y_lo), z: 8, core: 2. Of those that a mesh axis runs over, the one named last changes fastest.
Arguments:
- queries: bfloat16 [32, 2048, 128], P('row', 'col'), may hold values from -6.5 to 6.5
- keys: bfloat16 [32, 2048, 128], P('row', 'col'), may hold values from -6.5 to 6.5
- values: bfloat16 [32, 2048, 128], P('row', 'col'), may hold values from -6 to 6
- gate: bfloat16 [32, 2048, 128], P('row', 'col'), may hold values from -6 to 6
- bias: bfloat16 [4, 2048, 2048], P(None, 'col'), may hold values from -7.5 to 7.5
- grad_out: bfloat16 [32, 2048, 128], P('row', 'col'), may hold values from -6 to 6
- block_mask: int32 [16, 16], replicated, may hold values from 0 to 1, as said below
Outputs:
- query_grad: bfloat16 [32, 2048, 128], P('row', 'col')
- key_grad: bfloat16 [32, 2048, 128], P('row', 'col')
- value_grad: bfloat16 [32, 2048, 128], P('row', 'col')
- gate_grad: bfloat16 [32, 2048, 128], P('row', 'col')
- bias_grad: float32 [4, 2048, 2048], P(None, 'col', 'row')
Inputs may be any that keep to these rules, and one draw needn't show every extreme that they name: `block_mask`: every diagonal block is 1.
All inputs are finite; a program needn't handle non-finite values.
Results may differ from a plain program's by a relative error of at most 0.02.
Values may be sent and summed in bfloat16 or wider, within the bound.
No kernel may reach another device: no remote copies, remote signals or barrier semaphores. Data moves between devices by JAX's collectives and lax.ppermute only.
A program may use at most 64 MiB of HBM per device.

v0:
```python
import math

import jax
import jax.numpy as jnp
from jax import lax
from jax.sharding import PartitionSpec as P

H = 4
DH = 32
BLK = 128


NEGATIVE = -1000000000.0


def block_flags(block_mask, first_row, row_count, key_block):
    block_ids = (first_row + jnp.arange(row_count, dtype=jnp.int32)) // BLK
    column = lax.dynamic_index_in_dim(block_mask, key_block, axis=1, keepdims=False)
    matching = block_ids[:, None] == jnp.arange(block_mask.shape[0], dtype=jnp.int32)[None, :]
    return jnp.sum(jnp.where(matching, column[None, :], 0), axis=1) > 0


def tile_scores(query_tile, key_tile, bias_tile, allowed, score_scale):
    products = jnp.einsum(
        "rjhd,rkhd->rhjk", query_tile, key_tile, preferred_element_type=jnp.float32
    )
    scores = products * score_scale + bias_tile.astype(jnp.float32)[None]
    return jnp.where(allowed[None, None, :, None], scores, NEGATIVE)


def tile_grads(
    query_tile, key_tile, value_tile, bias_tile, allowed, log_total, grad_dot, out_grad, score_scale
):
    scores = tile_scores(query_tile, key_tile, bias_tile, allowed, score_scale)
    weights = jnp.exp(scores - log_total[..., None])
    prob_grad = jnp.einsum(
        "rjhd,rkhd->rhjk", out_grad, value_tile, preferred_element_type=jnp.float32
    )
    return (weights, weights * (prob_grad - grad_dot[..., None]))


def local(queries, keys, values, gate, bias, grad_out, block_mask):
    slab_rows, local_cols, channels = queries.shape
    head_count = H
    head_size = DH
    score_scale = 1.0 / math.sqrt(head_size)
    col_start = lax.axis_index("col") * local_cols
    key_all, value_all = (
        lax.all_gather(keys, "col", axis=1, tiled=True),
        lax.all_gather(values, "col", axis=1, tiled=True),
    )
    all_cols = key_all.shape[1]
    blocks = all_cols // BLK
    query_heads = queries.reshape(slab_rows, local_cols, head_count, head_size)
    key_heads_all = key_all.reshape(slab_rows, all_cols, head_count, head_size)
    value_heads_all = value_all.reshape(slab_rows, all_cols, head_count, head_size)

    def key_slices(key_block):
        offset = key_block * BLK
        return (
            lax.dynamic_slice_in_dim(key_heads_all, offset, BLK, 1),
            lax.dynamic_slice_in_dim(value_heads_all, offset, BLK, 1),
            lax.dynamic_slice_in_dim(bias, offset, BLK, 2),
            block_flags(block_mask, col_start, local_cols, key_block),
        )

    def stats_step(key_block, carried):
        key_tile, value_tile, bias_tile, allowed = key_slices(key_block)

        def stats_update(state_in):
            row_top, row_mass = state_in
            scores = tile_scores(query_heads, key_tile, bias_tile, allowed, score_scale)
            new_top = jnp.maximum(row_top, jnp.max(scores, axis=3))
            row_mass = row_mass * jnp.exp(row_top - new_top) + jnp.sum(
                jnp.exp(scores - new_top[..., None]), axis=3
            )
            return (new_top, row_mass)

        return lax.cond(jnp.any(allowed), stats_update, lambda kept: kept, carried)

    stat_shape = (slab_rows, head_count, local_cols)
    row_top, row_mass = lax.fori_loop(
        0,
        blocks,
        stats_step,
        (jnp.full(stat_shape, -1e30, jnp.float32), jnp.zeros(stat_shape, jnp.float32)),
    )
    log_total = row_top + jnp.log(row_mass)

    def attend_step(key_block, carried):
        key_tile, value_tile, bias_tile, allowed = key_slices(key_block)

        def attend_update(running):
            scores = tile_scores(query_heads, key_tile, bias_tile, allowed, score_scale)
            probs = jnp.exp(scores - log_total[..., None]).astype(jnp.bfloat16)
            return running + jnp.einsum(
                "rhjk,rkhd->rjhd", probs, value_tile, preferred_element_type=jnp.float32
            )

        return lax.cond(jnp.any(allowed), attend_update, lambda kept: kept, carried)

    attended = lax.fori_loop(
        0,
        blocks,
        attend_step,
        jnp.zeros((slab_rows, local_cols, head_count, head_size), jnp.float32),
    )
    gate_sig = jax.nn.sigmoid(gate.astype(jnp.float32)).reshape(
        slab_rows, local_cols, head_count, head_size
    )
    cotangent = grad_out.astype(jnp.float32).reshape(slab_rows, local_cols, head_count, head_size)
    gate_grad = (
        (cotangent * attended * gate_sig * (1.0 - gate_sig))
        .astype(jnp.bfloat16)
        .reshape(slab_rows, local_cols, channels)
    )
    out_grad = (cotangent * gate_sig).astype(jnp.bfloat16)
    grad_dot = jnp.transpose(jnp.sum(out_grad.astype(jnp.float32) * attended, axis=3), (0, 2, 1))

    def grad_step(key_block, carried):
        key_tile, value_tile, bias_tile, allowed = key_slices(key_block)

        def grad_update(state_in):
            query_acc, bias_part, key_part, value_part = state_in
            weights, score_grad = tile_grads(
                query_heads,
                key_tile,
                value_tile,
                bias_tile,
                allowed,
                log_total,
                grad_dot,
                out_grad,
                score_scale,
            )
            score_grad_b = score_grad.astype(jnp.bfloat16)
            query_acc = query_acc + jnp.einsum(
                "rhjk,rkhd->rjhd", score_grad_b, key_tile, preferred_element_type=jnp.float32
            )
            offset = key_block * BLK
            bias_part = lax.dynamic_update_slice_in_dim(
                bias_part, jnp.sum(score_grad, axis=0), offset, 2
            )
            key_piece = jnp.einsum(
                "rhjk,rjhd->rkhd", score_grad_b, query_heads, preferred_element_type=jnp.float32
            )
            value_piece = jnp.einsum(
                "rhjk,rjhd->rkhd",
                weights.astype(jnp.bfloat16),
                out_grad,
                preferred_element_type=jnp.float32,
            )
            key_part = lax.dynamic_update_slice_in_dim(
                key_part, key_piece.reshape(slab_rows, BLK, channels), offset, 1
            )
            value_part = lax.dynamic_update_slice_in_dim(
                value_part, value_piece.reshape(slab_rows, BLK, channels), offset, 1
            )
            return (query_acc, bias_part, key_part, value_part)

        return lax.cond(jnp.any(allowed), grad_update, lambda kept: kept, carried)

    part_shape = (slab_rows, all_cols, channels)
    initial = (
        jnp.zeros((slab_rows, local_cols, head_count, head_size), jnp.float32),
        jnp.zeros((head_count, local_cols, all_cols), jnp.float32),
        jnp.zeros(part_shape, jnp.float32),
        jnp.zeros(part_shape, jnp.float32),
    )
    query_acc, bias_part, key_part, value_part = lax.fori_loop(0, blocks, grad_step, initial)
    key_sum, value_sum = (
        lax.psum_scatter(key_part, "col", scatter_dimension=1, tiled=True),
        lax.psum_scatter(value_part, "col", scatter_dimension=1, tiled=True),
    )
    key_grad = (key_sum * score_scale).astype(jnp.bfloat16)
    value_grad = value_sum.astype(jnp.bfloat16)
    bias_grad = lax.psum_scatter(bias_part, "row", scatter_dimension=2, tiled=True)
    query_grad = (
        (query_acc * score_scale).astype(jnp.bfloat16).reshape(slab_rows, local_cols, channels)
    )
    return (query_grad, key_grad, value_grad, gate_grad, bias_grad)


def solution(mesh):
    return jax.shard_map(
        local,
        mesh=mesh,
        in_specs=(
            P("row", "col", None),
            P("row", "col", None),
            P("row", "col", None),
            P("row", "col", None),
            P(None, "col", None),
            P("row", "col", None),
            P(),
        ),
        out_specs=(
            P("row", "col", None),
            P("row", "col", None),
            P("row", "col", None),
            P("row", "col", None),
            P(None, "col", "row"),
        ),
        check_vma=False,
    )
```

profile of v0, /device:TPU:8, one launch (start us, length us, event | category | flops | bytes accessed | tf_op | source)
XLA Modules:
  0.0 606.3 jit_solution(3435595489802957417)
XLA Ops:
  8.7 3.1 copy.84
  12.1 0.8 copy.80
  12.9 0.8 copy.79
  13.6 33.5 %all-gather.3.cloned.1.call-done = bf16[2,2048,128]{2,1,0:T(8,128)(2,1)} async-done(((bf16[2,128,128]{2,1,0:T(8,128)(2,1)}), bf16[2,2048,128]{2,1,0:T(8,128)(2,1)}) %all-gather.3.cloned.1.call-update) | async-done | bytes 1048592 | tf_op jit(solution)/shard_map/all_gather | solution.py:49
  47.1 1.5 copy.74
  48.6 25.6 %while.56 = (s32[]{:T(128)}, f32[2,4,128]{2,1,0:T(4,128)S(1)}, f32[2,4,128]{2,1,0:T(4,128)S(1)}, s32[]{:T(128)}, s32[16,16]{0,1:T(8,128)S(1)}, /*index=5*/bf16[2...) while((s32[]{:T(128)}, f32[2,4,128]{2,1,0:T(4,128)S(1)}, ...), condition=%wide.region_7.8_spmd, body=%wide.region_0.7_spmd.sunk | while | flops 9250950 | bytes 1891393 | solution.py:82
  74.2 9.4 %all-gather.5.cloned.1.call-done = bf16[2,2048,128]{2,1,0:T(8,128)(2,1)} async-done(((bf16[2,128,128]{2,1,0:T(8,128)(2,1)}), bf16[2,2048,128]{2,1,0:T(8,128)(2,1)}) %all-gather.5.cloned.1.call-update) | async-done | bytes 1048592 | tf_op jit(solution)/shard_map/all_gather | solution.py:50
  83.6 2.3 copy.78
  86.6 33.4 %while.57 = (s32[]{:T(128)}, f32[2,128,4,32]{1,3,2,0:T(8,128)}, s32[]{:T(128)}, s32[16,16]{0,1:T(8,128)S(1)}, bf16[2,2048,4,32]{1,3,2,0:T(8,128)(2,1)S(1)}, /*in...) while((s32[]{:T(128)}, f32[2,128,4,32]{1,3,2,0:T(8,128)}, ...), condition=%wide.region_13.14_spmd, body=%wide.region_8.13_spmd.sunk | while | flops 17539204 | bytes 1122349 | solution.py:102
  89.5 2.1 conditional.7
  89.5 2.1 fusion.14
  93.0 2.1 conditional.7
  93.0 2.1 fusion.14
  96.5 2.1 conditional.7
  96.5 2.1 fusion.14
  114.5 2.1 conditional.7
  114.5 2.1 fusion.14
  118.0 2.1 conditional.7
  118.0 2.1 fusion.14
  120.1 1.5 multiply_reduce_fusion
  121.6 2.2 broadcast_in_dim.201
  124.1 1.5 broadcast.279.clone
  125.6 46.0 %while.58 = (s32[]{:T(128)}, f32[2,128,4,32]{1,3,2,0:T(8,128)S(1)}, f32[4,128,2048]{1,2,0:T(8,128)}, f32[2,2048,128]{1,2,0:T(8,128)S(1)}, f32[2,2048,128]{1,2,0:...) while((s32[]{:T(128)}, f32[2,128,4,32]{1,3,2,0:T(8,128)S(1)}, ...), condition=%wide.region_21.22_spmd, body=%wide.region_15.21_spmd.sunk | while | flops 43163780 | bytes 5319889 | solution.py:170
  128.5 4.6 conditional.8
  128.5 0.9 dynamic-slice_convert_fusion.2
  129.8 1.2 fusion.49
  134.5 4.6 conditional.8
  134.6 0.9 dynamic-slice_convert_fusion.2
  135.8 1.2 fusion.49
  140.5 4.6 conditional.8
  140.6 0.9 dynamic-slice_convert_fusion.2
  141.8 1.2 fusion.49
  161.0 4.6 conditional.8
  161.1 0.9 dynamic-slice_convert_fusion.2
  162.3 1.2 fusion.49
  167.1 4.6 conditional.8
  167.1 0.9 dynamic-slice_convert_fusion.2
  168.4 1.2 fusion.49
  171.6 3.0 copy.86
  174.7 1.8 copy.85
  176.6 5.4 copy.87
  182.0 0.7 copy.88
  182.7 0.7 copy.89
  183.5 127.3 %reduce-scatter.6.cloned.1.call-done = f32[2,128,128]{2,1,0:T(8,128)} async-done(((f32[2,2048,128]{2,1,0:T(8,128)}), f32[2,128,128]{2,1,0:T(8,128)}) %reduce-scatter.6.cloned.1.call-update) | async-done | bytes 131088 | tf_op jit(solution)/shard_map/reduce_scatter | solution.py:173
  310.8 1.5 convert_element_type.99
  312.4 66.6 %reduce-scatter.4.cloned.1.call-done = f32[2,128,128]{2,1,0:T(8,128)} async-done(((f32[2,2048,128]{2,1,0:T(8,128)}), f32[2,128,128]{2,1,0:T(8,128)}) %reduce-scatter.4.cloned.1.call-update) | async-done | bytes 131088 | tf_op jit(solution)/shard_map/reduce_scatter | solution.py:172
  378.9 1.5 multiply_convert_fusion.1
  380.5 219.3 %reduce-scatter.8.cloned.1.call-done = f32[4,128,128]{2,1,0:T(8,128)} async-done(((f32[4,128,2048]{2,1,0:T(8,128)}), f32[4,128,128]{2,1,0:T(8,128)}) %reduce-scatter.8.cloned.1.call-update) | async-done | bytes 262160 | tf_op jit(solution)/shard_map/reduce_scatter | solution.py:177
  (325 shorter events, 56.0 us)
Async XLA Ops:
  7.2 39.9 %all-gather.3.cloned.1.call-start = ((), (), s32[]{:S(2)}) async-start(), calls=%async_computation.3 | async-start | bytes 1114112 | tf_op jit(solution)/shard_map/all_gather | solution.py:49
  7.9 75.7 %all-gather.5.cloned.1.call-start = ((), (), s32[]{:S(2)}) async-start(), calls=%async_computation.4 | async-start | bytes 1114112 | tf_op jit(solution)/shard_map/all_gather | solution.py:50
  8.7 302.2 %reduce-scatter.6.cloned.1.call-start = ((), (), s32[]{:S(2)}) async-start(), calls=%async_computation.6 | async-start | bytes 2228224 | tf_op jit(solution)/shard_map/reduce_scatter | solution.py:173
  8.7 3.1 copy-start.3
  8.7 3.3 copy-start.4
  8.7 3.3 copy-start.1
  8.7 4.1 copy-start.2
  120.1 1.5 copy-start
  174.6 204.3 %reduce-scatter.4.cloned.1.call-start = ((), (), s32[]{:S(2)}) async-start(), calls=%async_computation.5 | async-start | bytes 2228224 | tf_op jit(solution)/shard_map/reduce_scatter | solution.py:172
  176.5 423.3 %reduce-scatter.8.cloned.1.call-start = ((), (), s32[]{:S(2)}) async-start(), calls=%async_computation.7 | async-start | bytes 4456448 | tf_op jit(solution)/shard_map/reduce_scatter | solution.py:177
Sparse Core Ops, SparseCore 0:
  9.8 37.2 all-gather.2
  48.9 34.6 all-gather.4
  174.7 136.0 reduce-scatter.5
  313.2 65.6 reduce-scatter.3
  383.4 216.3 reduce-scatter.7
where the time goes:
time: 609 us; the launch traced here: 606 us
  waiting for transfers between devices  458 us (75%)
  other arithmetic  45.4 us (7%)
  loops' own time  34 us (6%)
  local copies, waits for them, and re-layouts  32.6 us (5%)
  matrix products  22.7 us (4%)
  between operations  13.9 us (2%)
    reduce_scatter x1, waiting for transfers between devices, local(): lax.psum_scatter(bias_part, 'row', scatter_dimension=2, tiled=True)  219 us
    reduce_scatter x1, waiting for transfers between devices, local(): lax.psum_scatter(value_part, 'col', scatter_dimension=1, tiled=True)  127 us
    reduce_scatter x1, waiting for transfers between devices, local(): lax.psum_scatter(key_part, 'col', scatter_dimension=1, tiled=True)  66.6 us
    all_gather x1, waiting for transfers between devices, local(): lax.all_gather(keys, 'col', axis=1, tiled=True)  33.5 us
    gt x48, other arithmetic, block_flags(): return jnp.sum(jnp.where(matching, column[None, :], 0), axis=1) > 0  30.5 us
    while x5, local copies, waits for them, and re-layouts, local(): lax.fori_loop(0, blocks, grad_step, initial)  13.3 us
  transfers between devices with their start and end apart: 5, of which 5 were waited for; matrix products, arithmetic and copies ran while one was open for 5% of the time, Pallas kernels for 0%

commit v1 on v0

--- a/solution.py
+++ b/solution.py
@@ -121,7 +121,7 @@
         key_tile, value_tile, bias_tile, allowed = key_slices(key_block)
 
         def grad_update(state_in):
-            query_acc, bias_part, key_part, value_part = state_in
+            query_acc, bias_part, kv_part = state_in
             weights, score_grad = tile_grads(
                 query_heads,
                 key_tile,
@@ -139,7 +139,7 @@
             )
             offset = key_block * BLK
             bias_part = lax.dynamic_update_slice_in_dim(
-                bias_part, jnp.sum(score_grad, axis=0), offset, 2
+                bias_part, jnp.sum(score_grad, axis=0).astype(jnp.bfloat16), offset, 2
             )
             key_piece = jnp.einsum(
                 "rhjk,rjhd->rkhd", score_grad_b, query_heads, preferred_element_type=jnp.float32
@@ -150,31 +150,37 @@
                 out_grad,
                 preferred_element_type=jnp.float32,
             )
-            key_part = lax.dynamic_update_slice_in_dim(
-                key_part, key_piece.reshape(slab_rows, BLK, channels), offset, 1
-            )
-            value_part = lax.dynamic_update_slice_in_dim(
-                value_part, value_piece.reshape(slab_rows, BLK, channels), offset, 1
-            )
-            return (query_acc, bias_part, key_part, value_part)
+            piece = jnp.concatenate(
+                (
+                    key_piece.reshape(slab_rows, BLK, channels),
+                    value_piece.reshape(slab_rows, BLK, channels),
+                ),
+                axis=2,
+            ).astype(jnp.bfloat16)
+            kv_part = lax.dynamic_update_slice_in_dim(kv_part, piece, offset, 1)
+            return (query_acc, bias_part, kv_part)
 
         return lax.cond(jnp.any(allowed), grad_update, lambda kept: kept, carried)
 
-    part_shape = (slab_rows, all_cols, channels)
     initial = (
         jnp.zeros((slab_rows, local_cols, head_count, head_size), jnp.float32),
-        jnp.zeros((head_count, local_cols, all_cols), jnp.float32),
-        jnp.zeros(part_shape, jnp.float32),
-        jnp.zeros(part_shape, jnp.float32),
-    )
-    query_acc, bias_part, key_part, value_part = lax.fori_loop(0, blocks, grad_step, initial)
-    key_sum, value_sum = (
-        lax.psum_scatter(key_part, "col", scatter_dimension=1, tiled=True),
-        lax.psum_scatter(value_part, "col", scatter_dimension=1, tiled=True),
-    )
-    key_grad = (key_sum * score_scale).astype(jnp.bfloat16)
-    value_grad = value_sum.astype(jnp.bfloat16)
-    bias_grad = lax.psum_scatter(bias_part, "row", scatter_dimension=2, tiled=True)
+        jnp.zeros((head_count, local_cols, all_cols), jnp.bfloat16),
+        jnp.zeros((slab_rows, all_cols, 2 * channels), jnp.bfloat16),
+    )
+    query_acc, bias_part, kv_part = lax.fori_loop(0, blocks, grad_step, initial)
+    col_count = all_cols // local_cols
+    kv_moved = lax.all_to_all(
+        kv_part.reshape(slab_rows, col_count, local_cols, 2 * channels), "col", 1, 1, tiled=True
+    )
+    kv_sum = jnp.sum(kv_moved.astype(jnp.float32), axis=1)
+    key_grad = (kv_sum[..., :channels] * score_scale).astype(jnp.bfloat16)
+    value_grad = kv_sum[..., channels:].astype(jnp.bfloat16)
+    row_count = lax.axis_size("row")
+    row_keys = all_cols // row_count
+    bias_moved = lax.all_to_all(
+        bias_part.reshape(head_count, local_cols, row_count, row_keys), "row", 2, 2, tiled=True
+    )
+    bias_grad = jnp.sum(bias_moved.astype(jnp.float32), axis=2)
     query_grad = (
         (query_acc * score_scale).astype(jnp.bfloat16).reshape(slab_rows, local_cols, channels)
     )

time: 609 us -> 344 us (0.56)
  waiting for transfers between devices: 458 us -> 110 us
  matrix products: 22.7 us -> 72.2 us
  other arithmetic: 45.4 us -> 68.7 us
  starting transfers between devices: 0.2 us -> 13.4 us
    reduce_scatter x3 -> x0, waiting for transfers between devices: 413 us -> none  [the longest x1 219 us: local(): lax.psum_scatter(bias_part, 'row', scatter_dimension=2, tiled=True)]
    all_to_all x0 -> x2, waiting for transfers between devices: none -> 71.1 us  [the longest x1 47.4 us: local(): lax.all_to_all(bias_part.reshape(head_count, local_cols, row_count, row_k...]
    dot_general x5 -> x16, matrix products: 10.3 us -> 32.9 us  [attend_update(): jnp.einsum('rhjk,rkhd->rjhd', probs, value_tile, preferred_element_type=j...]
    all_to_all x0 -> x2, starting transfers between devices: none -> 13.3 us  [the longest x1 8.67 us: local(): lax.all_to_all(bias_part.reshape(head_count, local_cols, row_count, row_k...]
    dot_general x5 -> x16, matrix products: 5.81 us -> 18.2 us  [tile_grads(): jnp.einsum('rjhd,rkhd->rhjk', out_grad, value_tile, preferred_element_typ...]
    dynamic_update_slice x0 -> x16, other arithmetic: none -> 11.3 us  [grad_update(): kv_part = lax.dynamic_update_slice_in_dim(kv_part, piece, offset, 1)]
    convert_element_type x15 -> x48, other arithmetic: 4.92 us -> 15.7 us  [tile_scores(): scores = products * score_scale + bias_tile.astype(jnp.float32)[None]]
    reshape x0 -> x2, local copies, waits for them, and re-layouts: none -> 7.92 us  [the longest x1 3.96 us: local(): bias_part.reshape(head_count, local_cols, row_count, row_keys)]
  transfers between devices with their start and end apart: 5 -> 4, of which waited for: 5 -> 4; matrix products, arithmetic and copies ran while one was open for 5% -> 10% of each run, Pallas kernels for 0% -> 0%
where the time goes in v1:
time: 344 us; the launch traced here: 342 us
  waiting for transfers between devices  110 us (32%)
  matrix products  72.2 us (21%)
  other arithmetic  68.7 us (20%)
  loops' own time  34.6 us (10%)
  local copies, waits for them, and re-layouts  28.7 us (8%)
  between operations  14.2 us (4%)
  starting transfers between devices  13.4 us (4%)
    all_to_all x1, waiting for transfers between devices, local(): lax.all_to_all(bias_part.reshape(head_count, local_cols, row_count, row_k...  47.4 us
    all_gather x1, waiting for transfers between devices, local(): lax.all_gather(keys, 'col', axis=1, tiled=True)  33.5 us
    dot_general x16, matrix products, attend_update(): jnp.einsum('rhjk,rkhd->rjhd', probs, value_tile, preferred_element_type=j...  32.9 us
    gt x48, other arithmetic, block_flags(): return jnp.sum(jnp.where(matching, column[None, :], 0), axis=1) > 0  30.5 us
    all_to_all x1, waiting for transfers between devices, local(): lax.all_to_all(kv_part.reshape(slab_rows, col_count, local_cols, 2 * chan...  23.7 us
    dot_general x16, matrix products, tile_grads(): jnp.einsum('rjhd,rkhd->rhjk', out_grad, value_tile, preferred_element_typ...  18.2 us
    convert_element_type x48, other arithmetic, tile_scores(): scores = products * score_scale + bias_tile.astype(jnp.float32)[None]  15.7 us
    dynamic_update_slice x16, other arithmetic, grad_update(): kv_part = lax.dynamic_update_slice_in_dim(kv_part, piece, offset, 1)  11.3 us
  transfers between devices with their start and end apart: 4, of which 4 were waited for; matrix products, arithmetic and copies ran while one was open for 10% of the time, Pallas kernels for 0%

profile of v1, /device:TPU:8, one launch (start us, length us, event | category | flops | bytes accessed | tf_op | source)
XLA Modules:
  0.0 341.8 jit_solution(8592080000824858144)
XLA Ops:
  8.7 3.1 copy.103
  13.6 33.5 %all-gather.3.cloned.1.call-done = bf16[2,2048,128]{2,1,0:T(8,128)(2,1)} async-done(((bf16[2,128,128]{2,1,0:T(8,128)(2,1)}), bf16[2,2048,128]{2,1,0:T(8,128)(2,1)}) %all-gather.3.cloned.1.call-update) | async-done | bytes 1048592 | tf_op jit(solution)/shard_map/all_gather | solution.py:49
  48.6 31.0 %while.54 = (s32[]{:T(128)}, f32[2,4,128]{2,1,0:T(4,128)S(1)}, f32[2,4,128]{2,1,0:T(4,128)S(1)}, s32[]{:T(128)}, s32[16,16]{0,1:T(8,128)S(1)}, /*index=5*/bf16[2...) while((s32[]{:T(128)}, f32[2,4,128]{2,1,0:T(4,128)S(1)}, ...), condition=%wide.region_7.8_spmd, body=%wide.region_0.7_spmd.sunk | while | flops 9250950 | bytes 1891393 | solution.py:82
  79.6 4.0 %all-gather.5.cloned.1.call-done = bf16[2,2048,128]{2,1,0:T(8,128)(2,1)} async-done(((bf16[2,128,128]{2,1,0:T(8,128)(2,1)}), bf16[2,2048,128]{2,1,0:T(8,128)(2,1)}) %all-gather.5.cloned.1.call-update) | async-done | bytes 1048592 | tf_op jit(solution)/shard_map/all_gather | solution.py:50
  83.6 2.3 copy.97
  86.6 56.2 %while.55 = (s32[]{:T(128)}, f32[2,128,4,32]{1,3,2,0:T(8,128)}, s32[]{:T(128)}, s32[16,16]{0,1:T(8,128)S(1)}, bf16[2,2048,4,32]{1,3,2,0:T(8,128)(2,1)S(1)}, /*in...) while((s32[]{:T(128)}, f32[2,128,4,32]{1,3,2,0:T(8,128)}, ...), condition=%wide.region_13.14_spmd, body=%wide.region_8.13_spmd.sunk | while | flops 17539204 | bytes 1122349 | solution.py:102
  88.0 2.1 conditional.7
  91.5 2.1 conditional.7
  95.0 2.1 conditional.7
  98.5 2.1 conditional.7
  102.0 2.1 conditional.7
  102.1 2.1 fusion.14
  105.5 2.1 conditional.7
  109.0 2.1 conditional.7
  112.6 2.1 conditional.7
  116.1 2.1 conditional.7
  119.6 2.1 conditional.7
  123.1 2.1 conditional.7
  126.6 2.1 conditional.7
  130.1 2.1 conditional.7
  130.2 2.1 fusion.14
  133.6 2.1 conditional.7
  137.1 2.1 conditional.7
  140.6 2.1 conditional.7
  146.2 84.5 %while.56 = (s32[]{:T(128)}, f32[2,128,4,32]{1,3,2,0:T(8,128)S(1)}, bf16[4,128,2048]{1,2,0:T(8,128)(2,1)S(1)}, bf16[2,2048,256]{1,2,0:T(8,128)(2,1)}, s32[]{:T(1...) while((s32[]{:T(128)}, f32[2,128,4,32]{1,3,2,0:T(8,128)S(1)}, ...), condition=%wide.region_21.22_spmd, body=%wide.region_15.21_spmd.sunk | while | flops 43491460 | bytes 4533425 | solution.py:170
  147.6 3.9 %conditional.8 = ((f32[2,128,4,32]{1,3,2,0:T(8,128)S(1)}, bf16[4,128,2048]{1,2,0:T(8,128)(2,1)S(1)}, bf16[2,2048,256]{1,2,0:T(8,128)(2,1)})) conditional(s32[]{:T(128)} %convert_element_type.149, (f32[2,128,4,32]{1,3,2,0:T(8,128)S(1)}, bf16[4,128,2048]{1,2,0:T(8,128)(2,1)S(1)}, bf16[2,2048,256]{1,2,0:T(8,128)(2,1)}) %tuple.209, ...), branch_computations={%region_18.18_spmd, %region_19.20_spmd} | conditional | flops 43483140 | bytes 4530790 | solution.py:163
  152.9 3.8 %conditional.8 = ((f32[2,128,4,32]{1,3,2,0:T(8,128)S(1)}, bf16[4,128,2048]{1,2,0:T(8,128)(2,1)S(1)}, bf16[2,2048,256]{1,2,0:T(8,128)(2,1)})) conditional(s32[]{:T(128)} %convert_element_type.149, (f32[2,128,4,32]{1,3,2,0:T(8,128)S(1)}, bf16[4,128,2048]{1,2,0:T(8,128)(2,1)S(1)}, bf16[2,2048,256]{1,2,0:T(8,128)(2,1)}) %tuple.209, ...), branch_computations={%region_18.18_spmd, %region_19.20_spmd} | conditional | flops 43483140 | bytes 4530790 | solution.py:163
  158.2 3.8 %conditional.8 = ((f32[2,128,4,32]{1,3,2,0:T(8,128)S(1)}, bf16[4,128,2048]{1,2,0:T(8,128)(2,1)S(1)}, bf16[2,2048,256]{1,2,0:T(8,128)(2,1)})) conditional(s32[]{:T(128)} %convert_element_type.149, (f32[2,128,4,32]{1,3,2,0:T(8,128)S(1)}, bf16[4,128,2048]{1,2,0:T(8,128)(2,1)S(1)}, bf16[2,2048,256]{1,2,0:T(8,128)(2,1)}) %tuple.209, ...), branch_computations={%region_18.18_spmd, %region_19.20_spmd} | conditional | flops 43483140 | bytes 4530790 | solution.py:163
  163.4 3.8 %conditional.8 = ((f32[2,128,4,32]{1,3,2,0:T(8,128)S(1)}, bf16[4,128,2048]{1,2,0:T(8,128)(2,1)S(1)}, bf16[2,2048,256]{1,2,0:T(8,128)(2,1)})) conditional(s32[]{:T(128)} %convert_element_type.149, (f32[2,128,4,32]{1,3,2,0:T(8,128)S(1)}, bf16[4,128,2048]{1,2,0:T(8,128)(2,1)S(1)}, bf16[2,2048,256]{1,2,0:T(8,128)(2,1)}) %tuple.209, ...), branch_computations={%region_18.18_spmd, %region_19.20_spmd} | conditional | flops 43483140 | bytes 4530790 | solution.py:163
  168.7 3.8 %conditional.8 = ((f32[2,128,4,32]{1,3,2,0:T(8,128)S(1)}, bf16[4,128,2048]{1,2,0:T(8,128)(2,1)S(1)}, bf16[2,2048,256]{1,2,0:T(8,128)(2,1)})) conditional(s32[]{:T(128)} %convert_element_type.149, (f32[2,128,4,32]{1,3,2,0:T(8,128)S(1)}, bf16[4,128,2048]{1,2,0:T(8,128)(2,1)S(1)}, bf16[2,2048,256]{1,2,0:T(8,128)(2,1)}) %tuple.209, ...), branch_computations={%region_18.18_spmd, %region_19.20_spmd} | conditional | flops 43483140 | bytes 4530790 | solution.py:163
  174.0 3.8 %conditional.8 = ((f32[2,128,4,32]{1,3,2,0:T(8,128)S(1)}, bf16[4,128,2048]{1,2,0:T(8,128)(2,1)S(1)}, bf16[2,2048,256]{1,2,0:T(8,128)(2,1)})) conditional(s32[]{:T(128)} %convert_element_type.149, (f32[2,128,4,32]{1,3,2,0:T(8,128)S(1)}, bf16[4,128,2048]{1,2,0:T(8,128)(2,1)S(1)}, bf16[2,2048,256]{1,2,0:T(8,128)(2,1)}) %tuple.209, ...), branch_computations={%region_18.18_spmd, %region_19.20_spmd} | conditional | flops 43483140 | bytes 4530790 | solution.py:163
  179.3 3.8 %conditional.8 = ((f32[2,128,4,32]{1,3,2,0:T(8,128)S(1)}, bf16[4,128,2048]{1,2,0:T(8,128)(2,1)S(1)}, bf16[2,2048,256]{1,2,0:T(8,128)(2,1)})) conditional(s32[]{:T(128)} %convert_element_type.149, (f32[2,128,4,32]{1,3,2,0:T(8,128)S(1)}, bf16[4,128,2048]{1,2,0:T(8,128)(2,1)S(1)}, bf16[2,2048,256]{1,2,0:T(8,128)(2,1)}) %tuple.209, ...), branch_computations={%region_18.18_spmd, %region_19.20_spmd} | conditional | flops 43483140 | bytes 4530790 | solution.py:163
  184.6 3.8 %conditional.8 = ((f32[2,128,4,32]{1,3,2,0:T(8,128)S(1)}, bf16[4,128,2048]{1,2,0:T(8,128)(2,1)S(1)}, bf16[2,2048,256]{1,2,0:T(8,128)(2,1)})) conditional(s32[]{:T(128)} %convert_element_type.149, (f32[2,128,4,32]{1,3,2,0:T(8,128)S(1)}, bf16[4,128,2048]{1,2,0:T(8,128)(2,1)S(1)}, bf16[2,2048,256]{1,2,0:T(8,128)(2,1)}) %tuple.209, ...), branch_computations={%region_18.18_spmd, %region_19.20_spmd} | conditional | flops 43483140 | bytes 4530790 | solution.py:163
  189.8 3.8 %conditional.8 = ((f32[2,128,4,32]{1,3,2,0:T(8,128)S(1)}, bf16[4,128,2048]{1,2,0:T(8,128)(2,1)S(1)}, bf16[2,2048,256]{1,2,0:T(8,128)(2,1)})) conditional(s32[]{:T(128)} %convert_element_type.149, (f32[2,128,4,32]{1,3,2,0:T(8,128)S(1)}, bf16[4,128,2048]{1,2,0:T(8,128)(2,1)S(1)}, bf16[2,2048,256]{1,2,0:T(8,128)(2,1)}) %tuple.209, ...), branch_computations={%region_18.18_spmd, %region_19.20_spmd} | conditional | flops 43483140 | bytes 4530790 | solution.py:163
  195.1 3.8 %conditional.8 = ((f32[2,128,4,32]{1,3,2,0:T(8,128)S(1)}, bf16[4,128,2048]{1,2,0:T(8,128)(2,1)S(1)}, bf16[2,2048,256]{1,2,0:T(8,128)(2,1)})) conditional(s32[]{:T(128)} %convert_element_type.149, (f32[2,128,4,32]{1,3,2,0:T(8,128)S(1)}, bf16[4,128,2048]{1,2,0:T(8,128)(2,1)S(1)}, bf16[2,2048,256]{1,2,0:T(8,128)(2,1)}) %tuple.209, ...), branch_computations={%region_18.18_spmd, %region_19.20_spmd} | conditional | flops 43483140 | bytes 4530790 | solution.py:163
  200.4 3.8 %conditional.8 = ((f32[2,128,4,32]{1,3,2,0:T(8,128)S(1)}, bf16[4,128,2048]{1,2,0:T(8,128)(2,1)S(1)}, bf16[2,2048,256]{1,2,0:T(8,128)(2,1)})) conditional(s32[]{:T(128)} %convert_element_type.149, (f32[2,128,4,32]{1,3,2,0:T(8,128)S(1)}, bf16[4,128,2048]{1,2,0:T(8,128)(2,1)S(1)}, bf16[2,2048,256]{1,2,0:T(8,128)(2,1)}) %tuple.209, ...), branch_computations={%region_18.18_spmd, %region_19.20_spmd} | conditional | flops 43483140 | bytes 4530790 | solution.py:163
  205.6 3.8 %conditional.8 = ((f32[2,128,4,32]{1,3,2,0:T(8,128)S(1)}, bf16[4,128,2048]{1,2,0:T(8,128)(2,1)S(1)}, bf16[2,2048,256]{1,2,0:T(8,128)(2,1)})) conditional(s32[]{:T(128)} %convert_element_type.149, (f32[2,128,4,32]{1,3,2,0:T(8,128)S(1)}, bf16[4,128,2048]{1,2,0:T(8,128)(2,1)S(1)}, bf16[2,2048,256]{1,2,0:T(8,128)(2,1)}) %tuple.209, ...), branch_computations={%region_18.18_spmd, %region_19.20_spmd} | conditional | flops 43483140 | bytes 4530790 | solution.py:163
  210.9 3.9 %conditional.8 = ((f32[2,128,4,32]{1,3,2,0:T(8,128)S(1)}, bf16[4,128,2048]{1,2,0:T(8,128)(2,1)S(1)}, bf16[2,2048,256]{1,2,0:T(8,128)(2,1)})) conditional(s32[]{:T(128)} %convert_element_type.149, (f32[2,128,4,32]{1,3,2,0:T(8,128)S(1)}, bf16[4,128,2048]{1,2,0:T(8,128)(2,1)S(1)}, bf16[2,2048,256]{1,2,0:T(8,128)(2,1)}) %tuple.209, ...), branch_computations={%region_18.18_spmd, %region_19.20_spmd} | conditional | flops 43483140 | bytes 4530790 | solution.py:163
  216.2 3.9 %conditional.8 = ((f32[2,128,4,32]{1,3,2,0:T(8,128)S(1)}, bf16[4,128,2048]{1,2,0:T(8,128)(2,1)S(1)}, bf16[2,2048,256]{1,2,0:T(8,128)(2,1)})) conditional(s32[]{:T(128)} %convert_element_type.149, (f32[2,128,4,32]{1,3,2,0:T(8,128)S(1)}, bf16[4,128,2048]{1,2,0:T(8,128)(2,1)S(1)}, bf16[2,2048,256]{1,2,0:T(8,128)(2,1)}) %tuple.209, ...), branch_computations={%region_18.18_spmd, %region_19.20_spmd} | conditional | flops 43483140 | bytes 4530790 | solution.py:163
  221.5 3.8 %conditional.8 = ((f32[2,128,4,32]{1,3,2,0:T(8,128)S(1)}, bf16[4,128,2048]{1,2,0:T(8,128)(2,1)S(1)}, bf16[2,2048,256]{1,2,0:T(8,128)(2,1)})) conditional(s32[]{:T(128)} %convert_element_type.149, (f32[2,128,4,32]{1,3,2,0:T(8,128)S(1)}, bf16[4,128,2048]{1,2,0:T(8,128)(2,1)S(1)}, bf16[2,2048,256]{1,2,0:T(8,128)(2,1)}) %tuple.209, ...), branch_computations={%region_18.18_spmd, %region_19.20_spmd} | conditional | flops 43483140 | bytes 4530790 | solution.py:163
  226.8 3.9 %conditional.8 = ((f32[2,128,4,32]{1,3,2,0:T(8,128)S(1)}, bf16[4,128,2048]{1,2,0:T(8,128)(2,1)S(1)}, bf16[2,2048,256]{1,2,0:T(8,128)(2,1)})) conditional(s32[]{:T(128)} %convert_element_type.149, (f32[2,128,4,32]{1,3,2,0:T(8,128)S(1)}, bf16[4,128,2048]{1,2,0:T(8,128)(2,1)S(1)}, bf16[2,2048,256]{1,2,0:T(8,128)(2,1)}) %tuple.209, ...), branch_computations={%region_18.18_spmd, %region_19.20_spmd} | conditional | flops 43483140 | bytes 4530790 | solution.py:163
  230.7 4.6 %copy.104 = bf16[2,2048,256]{2,1,0:T(8,128)(2,1)} copy(bf16[2,2048,256]{1,2,0:T(8,128)(2,1)} %get-tuple-element.1186) | data formatting | bytes 4194304 | tf_op jit(solution)/shard_map/while | solution.py:170
  235.3 4.0 %copy.105 = bf16[2,16,128,256]{2,3,0,1:T(8,128)(2,1)} copy(bf16[2,16,128,256]{3,2,1,0:T(8,128)(2,1)} %bitcast.94) | data formatting | bytes 4194304 | tf_op jit(solution)/shard_map/reshape | solution.py:173
  239.2 4.6 %all-to-all-start = ((bf16[2,16,128,256]{2,3,0,1:T(8,128)(2,1)}), bf16[2,16,128,256]{2,3,0,1:T(8,128)(2,1)S(1)}, u32[]{:S(2)}, u32[]{:S(2)}) async-start(bf16[2,16,128,256]{2,3,0,1:T(8,128)(2,1)} %copy.105), calls=%async_computation | async-start | bytes 4194304 | tf_op jit(solution)/shard_map/all_to_all | solution.py:172
  243.8 4.0 %copy.107 = bf16[4,128,16,128]{3,1,0,2:T(8,128)(2,1)} copy(bf16[4,128,16,128]{1,3,2,0:T(8,128)(2,1)} %bitcast.93) | data formatting | bytes 4194304 | tf_op jit(solution)/shard_map/reshape | solution.py:181
  247.8 23.7 %all-to-all-done = bf16[2,16,128,256]{2,3,0,1:T(8,128)(2,1)S(1)} async-done(((bf16[2,16,128,256]{2,3,0,1:T(8,128)(2,1)}), bf16[2,16,128,256]{2,3,0,1:T(8,128)(2,1)S(1)}, u32[]{:S(2)}, u32[]{:S(2)}) %all-to-all-start) | async-done | bytes 2097184 | tf_op jit(solution)/shard_map/all_to_all | solution.py:172
  272.8 8.7 %all-to-all-start.1 = ((bf16[4,128,16,128]{3,1,0,2:T(8,128)(2,1)}), bf16[4,128,16,128]{3,1,0,2:T(8,128)(2,1)S(1)}, u32[]{:S(2)}, u32[]{:S(2)}) async-start(bf16[4,128,16,128]{3,1,0,2:T(8,128)(2,1)} %copy.107), calls=%async_computation.1 | async-start | bytes 4194304 | tf_op jit(solution)/shard_map/all_to_all | solution.py:180
  286.5 47.4 %all-to-all-done.1 = bf16[4,128,16,128]{3,1,0,2:T(8,128)(2,1)S(1)} async-done(((bf16[4,128,16,128]{3,1,0,2:T(8,128)(2,1)}), bf16[4,128,16,128]{3,1,0,2:T(8,128)(2,1)S(1)}, u32[]{:S(2)}, u32[]{:S(2)}) %all-to-all-start.1) | async-done | bytes 2097184 | tf_op jit(solution)/shard_map/all_to_all | solution.py:180
  (503 shorter events, 157.1 us)
Async XLA Ops:
  7.2 39.9 %all-gather.3.cloned.1.call-start = ((), (), s32[]{:S(2)}) async-start(), calls=%async_computation.2 | async-start | bytes 1114112 | tf_op jit(solution)/shard_map/all_gather | solution.py:49
  7.9 75.7 %all-gather.5.cloned.1.call-start = ((), (), s32[]{:S(2)}) async-start(), calls=%async_computation.3 | async-start | bytes 1114112 | tf_op jit(solution)/shard_map/all_gather | solution.py:50
  8.7 3.1 copy-start.5
  8.7 3.3 copy-start.6
  8.7 3.3 copy-start.3
  8.7 4.1 %copy-start.4 = (bf16[2,128,128]{2,1,0:T(8,128)(2,1)S(1)}, bf16[2,128,128]{2,1,0:T(8,128)(2,1)}, u32[]{:S(2)}) copy-start(bf16[2,128,128]{2,1,0:T(8,128)(2,1)} %param.24) | copy-start | bytes 196612
  142.8 1.5 copy-start.2
  230.7 4.6 %copy-start.1 = (bf16[4,128,2048]{1,2,0:T(8,128)(2,1)}, bf16[4,128,2048]{1,2,0:T(8,128)(2,1)S(1)}, u32[]{:S(2)}) copy-start(bf16[4,128,2048]{1,2,0:T(8,128)(2,1)S(1)} %get-tuple-element.1187) | copy-start | bytes 6291460
  239.2 32.3 %all-to-all-start = ((bf16[2,16,128,256]{2,3,0,1:T(8,128)(2,1)}), bf16[2,16,128,256]{2,3,0,1:T(8,128)(2,1)S(1)}, u32[]{:S(2)}, u32[]{:S(2)}) async-start(bf16[2,16,128,256]{2,3,0,1:T(8,128)(2,1)} %copy.105), calls=%async_computation | async-start | bytes 4194304 | tf_op jit(solution)/shard_map/all_to_all | solution.py:172
  271.5 1.4 copy-start
  272.8 61.1 %all-to-all-start.1 = ((bf16[4,128,16,128]{3,1,0,2:T(8,128)(2,1)}), bf16[4,128,16,128]{3,1,0,2:T(8,128)(2,1)S(1)}, u32[]{:S(2)}, u32[]{:S(2)}) async-start(bf16[4,128,16,128]{3,1,0,2:T(8,128)(2,1)} %copy.107), calls=%async_computation.1 | async-start | bytes 4194304 | tf_op jit(solution)/shard_map/all_to_all | solution.py:180
Sparse Core Ops, SparseCore 0:
  9.8 37.2 all-gather.2
  48.9 34.6 all-gather.4

commit v2 on v1

v2 whole, which is shorter than its diff:
```python
import math

import jax
import jax.numpy as jnp
from jax import lax
from jax.sharding import PartitionSpec as P

H = 4
DH = 32
BLK = 128


NEGATIVE = -1000000000.0


def local(queries, keys, values, gate, bias, grad_out, block_mask):
    slab_rows, local_cols, channels = queries.shape
    head_count = H
    head_size = DH
    score_scale = 1.0 / math.sqrt(head_size)
    col_start = lax.axis_index("col") * local_cols
    key_all = lax.all_gather(keys, "col", axis=1, tiled=True)
    value_all = lax.all_gather(values, "col", axis=1, tiled=True)
    all_cols = key_all.shape[1]
    query_heads = queries.reshape(slab_rows, local_cols, head_count, head_size)
    key_heads = key_all.reshape(slab_rows, all_cols, head_count, head_size)
    value_heads = value_all.reshape(slab_rows, all_cols, head_count, head_size)

    block_ids = (col_start + jnp.arange(local_cols, dtype=jnp.int32)) // BLK
    allowed = jnp.repeat(jnp.take(block_mask, block_ids, axis=0), BLK, axis=1) > 0

    products = jnp.einsum(
        "rjhd,rkhd->rhjk", query_heads, key_heads, preferred_element_type=jnp.float32
    )
    scores = products * score_scale + bias.astype(jnp.float32)[None]
    scores = jnp.where(allowed[None, None], scores, NEGATIVE)
    row_top = jnp.max(scores, axis=3, keepdims=True)
    log_total = row_top + jnp.log(jnp.sum(jnp.exp(scores - row_top), axis=3, keepdims=True))
    weights = jnp.exp(scores - log_total)
    probs = weights.astype(jnp.bfloat16)
    attended = jnp.einsum("rhjk,rkhd->rjhd", probs, value_heads, preferred_element_type=jnp.float32)

    gate_sig = jax.nn.sigmoid(gate.astype(jnp.float32)).reshape(
        slab_rows, local_cols, head_count, head_size
    )
    cotangent = grad_out.astype(jnp.float32).reshape(slab_rows, local_cols, head_count, head_size)
    gate_grad = (
        (cotangent * attended * gate_sig * (1.0 - gate_sig))
        .astype(jnp.bfloat16)
        .reshape(slab_rows, local_cols, channels)
    )
    out_grad = (cotangent * gate_sig).astype(jnp.bfloat16)
    grad_dot = jnp.transpose(jnp.sum(out_grad.astype(jnp.float32) * attended, axis=3), (0, 2, 1))

    prob_grad = jnp.einsum(
        "rjhd,rkhd->rhjk", out_grad, value_heads, preferred_element_type=jnp.float32
    )
    score_grad = weights * (prob_grad - grad_dot[..., None])
    score_grad_b = score_grad.astype(jnp.bfloat16)
    query_acc = jnp.einsum(
        "rhjk,rkhd->rjhd", score_grad_b, key_heads, preferred_element_type=jnp.float32
    )
    key_part = jnp.einsum(
        "rhjk,rjhd->rkhd", score_grad_b, query_heads, preferred_element_type=jnp.float32
    ).reshape(slab_rows, all_cols, channels)
    value_part = jnp.einsum(
        "rhjk,rjhd->rkhd", probs, out_grad, preferred_element_type=jnp.float32
    ).reshape(slab_rows, all_cols, channels)
    kv_part = jnp.concatenate((key_part, value_part), axis=2).astype(jnp.bfloat16)
    bias_part = jnp.sum(score_grad, axis=0).astype(jnp.bfloat16)

    col_count = all_cols // local_cols
    kv_moved = lax.all_to_all(
        kv_part.reshape(slab_rows, col_count, local_cols, 2 * channels), "col", 1, 1, tiled=True
    )
    kv_sum = jnp.sum(kv_moved.astype(jnp.float32), axis=1)
    key_grad = (kv_sum[..., :channels] * score_scale).astype(jnp.bfloat16)
    value_grad = kv_sum[..., channels:].astype(jnp.bfloat16)
    row_count = lax.axis_size("row")
    row_keys = all_cols // row_count
    bias_moved = lax.all_to_all(
        bias_part.reshape(head_count, local_cols, row_count, row_keys), "row", 2, 2, tiled=True
    )
    bias_grad = jnp.sum(bias_moved.astype(jnp.float32), axis=2)
    query_grad = (
        (query_acc * score_scale).astype(jnp.bfloat16).reshape(slab_rows, local_cols, channels)
    )
    return (query_grad, key_grad, value_grad, gate_grad, bias_grad)


def solution(mesh):
    return jax.shard_map(
        local,
        mesh=mesh,
        in_specs=(
            P("row", "col", None),
            P("row", "col", None),
            P("row", "col", None),
            P("row", "col", None),
            P(None, "col", None),
            P("row", "col", None),
            P(),
        ),
        out_specs=(
            P("row", "col", None),
            P("row", "col", None),
            P("row", "col", None),
            P("row", "col", None),
            P(None, "col", "row"),
        ),
        check_vma=False,
    )
```

time: 344 us -> 204 us (0.59)
  other arithmetic: 68.7 us -> 10.9 us
  matrix products: 72.2 us -> 20.4 us
  loops' own time: 34.6 us -> 0 us
  waiting for transfers between devices: 110 us -> 125 us
  local copies, waits for them, and re-layouts: 28.7 us -> 18.9 us
    dot_general x112 -> x6, matrix products: 72.2 us -> 20.4 us  [the longest x1 5.23 us: local(): jnp.einsum('rhjk,rkhd->rjhd', probs, value_heads, preferred_element_type=...]
    another operation x51 -> x0, loops' own time: 34.6 us -> none  [the longest x1 11 us: local(): query_acc, bias_part, kv_part = lax.fori_loop(0, blocks, grad_step, initial)]
    gt x48 -> x1, other arithmetic: 30.5 us -> 0.09 us  [local(): jnp.repeat(jnp.take(block_mask, block_ids, axis=0), BLK, axis=1) > 0]
    all_gather x2, waiting for transfers between devices: 37.5 us -> 58.5 us  [the longest x1 31 us: local(): key_all = lax.all_gather(keys, 'col', axis=1, tiled=True)]
    convert_element_type x49 -> x1, other arithmetic: 15.8 us -> 4.05 us  [local(): scores = products * score_scale + bias.astype(jnp.float32)[None]]
    dynamic_update_slice x16 -> x0, other arithmetic: 11.3 us -> none  [grad_update(): kv_part = lax.dynamic_update_slice_in_dim(kv_part, piece, offset, 1)]
    reshape x2 -> x0, local copies, waits for them, and re-layouts: 7.92 us -> none  [the longest x1 3.96 us: local(): bias_part.reshape(head_count, local_cols, row_count, row_keys)]
    while x3 -> x0, local copies, waits for them, and re-layouts: 7.75 us -> none  [local(): query_acc, bias_part, kv_part = lax.fori_loop(0, blocks, grad_step, initial)]
  transfers between devices with their start and end apart: 4 -> 4, of which waited for: 4 -> 4; matrix products, arithmetic and copies ran while one was open for 10% -> 15% of each run, Pallas kernels for 0% -> 0%
where the time goes in v2:
time: 204 us; the launch traced here: 203 us
  waiting for transfers between devices  125 us (61%)
  matrix products  20.4 us (10%)
  local copies, waits for them, and re-layouts  18.9 us (9%)
  between operations  14.2 us (7%)
  starting transfers between devices  13.6 us (7%)
  other arithmetic  10.9 us (5%)
    all_to_all x1, waiting for transfers between devices, local(): lax.all_to_all(bias_part.reshape(head_count, local_cols, row_count, row_k...  43.7 us
    all_gather x1, waiting for transfers between devices, local(): key_all = lax.all_gather(keys, 'col', axis=1, tiled=True)  31 us
    all_gather x1, waiting for transfers between devices, local(): value_all = lax.all_gather(values, 'col', axis=1, tiled=True)  27.5 us
    all_to_all x1, waiting for transfers between devices, local(): lax.all_to_all(kv_part.reshape(slab_rows, col_count, local_cols, 2 * chan...  21.4 us
    all_to_all x1, starting transfers between devices, local(): lax.all_to_all(bias_part.reshape(head_count, local_cols, row_count, row_k...  8.63 us
    unnamed x20, local copies, waits for them, and re-layouts  6.93 us
    convert_element_type x2, local copies, waits for them, and re-layouts, local(): bias_part = jnp.sum(score_grad, axis=0).astype(jnp.bfloat16)  6.44 us
    dot_general x1, matrix products, local(): jnp.einsum('rhjk,rkhd->rjhd', probs, value_heads, preferred_element_type=...  5.23 us
  transfers between devices with their start and end apart: 4, of which 4 were waited for; matrix products, arithmetic and copies ran while one was open for 15% of the time, Pallas kernels for 0%

profile of v2, /device:TPU:8, one launch (start us, length us, event | category | flops | bytes accessed | tf_op | source)
XLA Modules:
  0.0 203.1 jit_solution(969165539936813621)
XLA Ops:
  7.2 0.0 copy-start
  7.2 0.0 all-gather.3.cloned.1.call-start
  7.2 0.7 all-gather.3.cloned.1.call-update
  7.9 0.0 all-gather.5.cloned.1.call-start
  8.0 0.7 all-gather.5.cloned.1.call-update
  8.7 0.9 copy.54
  9.6 0.9 add_divide_fusion
  10.5 0.1 copy.55
  10.6 4.1 %convert_element_type.47 = f32[4,128,2048]{2,1,0:T(8,128)} convert(bf16[4,128,2048]{2,1,0:T(8,128)(2,1)} %param.11) | non-fusion elementwise | flops 1048576 | bytes 6291456 | tf_op jit(solution)/shard_map/convert_element_type | solution.py:35
  14.7 0.0 copy-done.5
  14.7 0.1 copy.52
  14.8 0.0 copy-done
  14.8 0.6 gather_fusion
  15.5 0.1 select_compare_fusion
  15.6 0.3 broadcast_in_dim.32
  15.9 0.1 copy.71
  16.1 31.0 %all-gather.3.cloned.1.call-done = bf16[2,2048,128]{2,1,0:T(8,128)(2,1)} async-done(((bf16[2,128,128]{2,1,0:T(8,128)(2,1)}), bf16[2,2048,128]{2,1,0:T(8,128)(2,1)}) %all-gather.3.cloned.1.call-update) | async-done | bytes 1048592 | tf_op jit(solution)/shard_map/all_gather | solution.py:22
  47.1 1.5 copy.53
  48.6 4.3 %fusion.14 = (f32[2,4,128]{2,1,0:T(4,128)S(1)}, f32[2,4,128,2048]{3,2,1,0:T(8,128)S(1)}) fusion(f32[4,128,2048]{2,1,0:T(8,128)} %convert_element_type.47, bf16[2,128,4,32]{1,3,2,0:T(8,128)(2,1)S(1)} %bitcast.59, bf16[2,2048,4,32]{1,3,2,0:T(8,128)(2,1)S(1)} %bitcast.48, pred[128,2048]{1,0:T(8,128)(4,1)S(1)} %bitcast.57), kind=kOutput, calls=%fused_computation.40 | convolution fusion | flops 142605312 | bytes 13963264 | tf_op jit(solution)/shard_map/rjhd,rkhd->rhjk/dot_general | solution.py:32
  52.9 1.3 exponential_reduce_fusion
  54.2 1.9 copy-done.1
  56.2 27.5 %all-gather.5.cloned.1.call-done = bf16[2,2048,128]{2,1,0:T(8,128)(2,1)} async-done(((bf16[2,128,128]{2,1,0:T(8,128)(2,1)}), bf16[2,2048,128]{2,1,0:T(8,128)(2,1)}) %all-gather.5.cloned.1.call-update) | async-done | bytes 1048592 | tf_op jit(solution)/shard_map/all_gather | solution.py:23
  83.7 1.5 copy.56
  85.1 0.0 copy-start.2
  85.2 5.2 %multiply_reduce_fusion = (f32[2,128,4]{1,2,0:T(4,128)S(1)}, bf16[2,128,4,32]{1,3,2,0:T(8,128)(2,1)S(1)}, bf16[2,128,4,32]{1,3,2,0:T(8,128)(2,1)S(1)}) fusion(f32[2,128,4,32]{1,3,2,0:T(8,128)S(1)} %bitcast.61, f32[2,128,4,32]{1,3,2,0:T(8,128)S(1)} %bitcast.62, bf16[2,2048,4,32]{1,3,2,0:T(8,128)(2,1)S(1)} %bitcast.50, f32[2,4,128,2048]{3,2,1,0:T(8,128)} %copy-done.1, ...), kind=kOutput, calls=%fused_computation.22 | convolution fusion | flops 138738688 | bytes 9838592 | tf_op jit(solution)/shard_map/rhjk,rkhd->rjhd/dot_general | solution.py:41
  90.4 0.5 copy-done.2
  90.9 1.6 convolution_convert_fusion.1
  92.5 4.8 %fusion.15 = (bf16[4,128,2048]{2,1,0:T(8,128)(2,1)}, bf16[2,4,128,2048]{3,2,1,0:T(8,128)(2,1)S(1)}) fusion(f32[2,4,128]{2,1,0:T(4,128)S(1)} %bitcast.70, bf16[2,128,4,32]{1,3,2,0:T(8,128)(2,1)S(1)} %get-tuple-element.31, bf16[2,2048,4,32]{1,3,2,0:T(8,128)(2,1)S(1)} %bitcast.51, f32[2,4,128,2048]{3,2,1,0:T(8,128)S(1)} %copy-done.2, f32[2,4,128]{2,1,0:T(4,128)S(1)} %bitcast.67), kind=kOutput, calls=%fused_computation.41 | convolution fusion | flops 143654912 | bytes 15802368 | tf_op jit(solution)/shard_map/rjhd,rkhd->rhjk/dot_general | solution.py:55
  97.3 0.2 copy.69
  97.6 0.3 copy.58
  97.9 0.7 convolution_convert_fusion
  98.5 0.7 copy-done.3
  99.3 0.2 copy.68
  99.5 0.3 copy.57
  99.8 1.6 pad_maximum_fusion
  101.4 4.9 %all-to-all-start = ((bf16[2,16,128,256]{2,3,0,1:T(8,128)(2,1)}), bf16[2,16,128,256]{2,3,0,1:T(8,128)(2,1)}, u32[]{:S(2)}, u32[]{:S(2)}) async-start(bf16[2,16,128,256]{2,3,0,1:T(8,128)(2,1)} %pad_maximum_fusion), calls=%async_computation | async-start | bytes 4194304 | tf_op jit(solution)/shard_map/all_to_all | solution.py:73
  106.3 2.5 %copy.60 = bf16[4,128,2048]{1,2,0:T(8,128)(2,1)} copy(bf16[4,128,2048]{2,1,0:T(8,128)(2,1)S(1)} %copy-done.4) | data formatting | bytes 4194304 | tf_op jit(solution)/shard_map/convert_element_type | solution.py:70
  108.8 3.9 %copy.61 = bf16[4,128,16,128]{3,1,0,2:T(8,128)(2,1)} copy(bf16[4,128,16,128]{1,3,2,0:T(8,128)(2,1)} %bitcast.52) | data formatting | bytes 4194304 | tf_op jit(solution)/shard_map/convert_element_type | solution.py:70
  112.7 21.4 %all-to-all-done = bf16[2,16,128,256]{2,3,0,1:T(8,128)(2,1)} async-done(((bf16[2,16,128,256]{2,3,0,1:T(8,128)(2,1)}), bf16[2,16,128,256]{2,3,0,1:T(8,128)(2,1)}, u32[]{:S(2)}, u32[]{:S(2)}) %all-to-all-start) | async-done | bytes 2097184 | tf_op jit(solution)/shard_map/all_to_all | solution.py:73
  134.2 8.6 %all-to-all-start.1 = ((bf16[4,128,16,128]{3,1,0,2:T(8,128)(2,1)}), bf16[4,128,16,128]{3,1,0,2:T(8,128)(2,1)S(1)}, u32[]{:S(2)}, u32[]{:S(2)}) async-start(bf16[4,128,16,128]{3,1,0,2:T(8,128)(2,1)} %copy.61), calls=%async_computation.1 | async-start | bytes 4194304 | tf_op jit(solution)/shard_map/all_to_all | solution.py:81
  142.8 3.7 %fusion.7 = bf16[2,4,128,32]{2,3,1,0:T(8,128)(2,1)S(1)} fusion(bf16[2,2048,4,32]{1,3,2,0:T(8,128)(2,1)S(1)} %bitcast.49, bf16[2,4,128,2048]{3,2,1,0:T(8,128)(2,1)} %copy-done.3), kind=kOutput, calls=%fused_computation.16 | convolution fusion | flops 134283264 | bytes 5308416 | tf_op jit(solution)/shard_map/rhjk,rkhd->rjhd/dot_general | solution.py:60
  146.5 0.8 copy.62
  147.3 0.7 copy.65
  148.0 1.9 convert_reduce_fusion.1
  150.0 0.7 copy.63
  150.8 0.7 copy.64
  151.5 43.7 %all-to-all-done.1 = bf16[4,128,16,128]{3,1,0,2:T(8,128)(2,1)S(1)} async-done(((bf16[4,128,16,128]{3,1,0,2:T(8,128)(2,1)}), bf16[4,128,16,128]{3,1,0,2:T(8,128)(2,1)S(1)}, u32[]{:S(2)}, u32[]{:S(2)}) %all-to-all-start.1) | async-done | bytes 2097184 | tf_op jit(solution)/shard_map/all_to_all | solution.py:81
  195.2 1.1 convert_reduce_fusion
  (11 shorter events, 0.1 us)
Async XLA Ops:
  7.2 7.7 %copy-start = (s32[16,16]{1,0:T(8,128)S(1)}, s32[16,16]{1,0:T(8,128)}, u32[]{:S(2)}) copy-start(s32[16,16]{1,0:T(8,128)} %param.13) | copy-start | bytes 3076
  7.2 7.5 %copy-start.5 = (bf16[2,128,128]{2,1,0:T(8,128)(2,1)S(1)}, bf16[2,128,128]{2,1,0:T(8,128)(2,1)}, u32[]{:S(2)}) copy-start(bf16[2,128,128]{2,1,0:T(8,128)(2,1)} %param.7) | copy-start | bytes 196612
  7.2 39.9 %all-gather.3.cloned.1.call-start = ((), (), s32[]{:S(2)}) async-start(), calls=%async_computation.2 | async-start | bytes 1114112 | tf_op jit(solution)/shard_map/all_gather | solution.py:22
  7.9 75.7 %all-gather.5.cloned.1.call-start = ((), (), s32[]{:S(2)}) async-start(), calls=%async_computation.3 | async-start | bytes 1114112 | tf_op jit(solution)/shard_map/all_gather | solution.py:23
  52.9 3.2 %copy-start.1 = (f32[2,4,128,2048]{3,2,1,0:T(8,128)}, f32[2,4,128,2048]{3,2,1,0:T(8,128)S(1)}, u32[]{:S(2)}) copy-start(f32[2,4,128,2048]{3,2,1,0:T(8,128)S(1)} %get-tuple-element.34) | copy-start | bytes 25165828
  85.1 5.8 %copy-start.2 = (f32[2,4,128,2048]{3,2,1,0:T(8,128)S(1)}, f32[2,4,128,2048]{3,2,1,0:T(8,128)}, u32[]{:S(2)}) copy-start(f32[2,4,128,2048]{3,2,1,0:T(8,128)} %copy-done.1) | copy-start | bytes 25165828
  97.3 1.9 copy-start.3
  99.8 6.5 %copy-start.4 = (bf16[4,128,2048]{2,1,0:T(8,128)(2,1)S(1)}, bf16[4,128,2048]{2,1,0:T(8,128)(2,1)}, u32[]{:S(2)}) copy-start(bf16[4,128,2048]{2,1,0:T(8,128)(2,1)} %get-tuple-element.35) | copy-start | bytes 6291460
  101.4 32.8 %all-to-all-start = ((bf16[2,16,128,256]{2,3,0,1:T(8,128)(2,1)}), bf16[2,16,128,256]{2,3,0,1:T(8,128)(2,1)}, u32[]{:S(2)}, u32[]{:S(2)}) async-start(bf16[2,16,128,256]{2,3,0,1:T(8,128)(2,1)} %pad_maximum_fusion), calls=%async_computation | async-start | bytes 4194304 | tf_op jit(solution)/shard_map/all_to_all | solution.py:73
  134.2 61.0 %all-to-all-start.1 = ((bf16[4,128,16,128]{3,1,0,2:T(8,128)(2,1)}), bf16[4,128,16,128]{3,1,0,2:T(8,128)(2,1)S(1)}, u32[]{:S(2)}, u32[]{:S(2)}) async-start(bf16[4,128,16,128]{3,1,0,2:T(8,128)(2,1)} %copy.61), calls=%async_computation.1 | async-start | bytes 4194304 | tf_op jit(solution)/shard_map/all_to_all | solution.py:81
Sparse Core Ops, SparseCore 0:
  9.8 37.2 all-gather.2
  48.9 34.6 all-gather.4

commit v3 on v2

--- a/solution.py
+++ b/solution.py
@@ -19,8 +19,9 @@
     head_size = DH
     score_scale = 1.0 / math.sqrt(head_size)
     col_start = lax.axis_index("col") * local_cols
-    key_all = lax.all_gather(keys, "col", axis=1, tiled=True)
-    value_all = lax.all_gather(values, "col", axis=1, tiled=True)
+    kv_all = lax.all_gather(jnp.concatenate((keys, values), axis=2), "col", axis=1, tiled=True)
+    key_all = kv_all[..., :channels]
+    value_all = kv_all[..., channels:]
     all_cols = key_all.shape[1]
     query_heads = queries.reshape(slab_rows, local_cols, head_count, head_size)
     key_heads = key_all.reshape(slab_rows, all_cols, head_count, head_size)

time: 204 us -> 173 us (0.85)
  waiting for transfers between devices: 125 us -> 103 us
  local copies, waits for them, and re-layouts: 18.9 us -> 15.4 us
  matrix products: 20.4 us -> 17.2 us
  other arithmetic: 10.9 us -> 8.26 us
    all_gather x2 -> x1, waiting for transfers between devices: 58.5 us -> 33.5 us  [local(): lax.all_gather(jnp.concatenate((keys, values), axis=2), 'col', axis=1, ti...]
    convert_element_type x0 -> x1, local copies, waits for them, and re-layouts: none -> 4.13 us  [local(): scores = products * score_scale + bias.astype(jnp.float32)[None]]
    convert_element_type x1 -> x0, other arithmetic: 4.05 us -> none  [local(): scores = products * score_scale + bias.astype(jnp.float32)[None]]
    convert_element_type x2 -> x1, local copies, waits for them, and re-layouts: 6.44 us -> 2.63 us  [local(): bias_part = jnp.sum(score_grad, axis=0).astype(jnp.bfloat16)]
    all_to_all x1, waiting for transfers between devices: 21.4 us -> 25.1 us  [local(): lax.all_to_all(kv_part.reshape(slab_rows, col_count, local_cols, 2 * chan...]
    dot_general x1, matrix products: 5.23 us -> 1.73 us  [local(): jnp.einsum('rhjk,rkhd->rjhd', probs, value_heads, preferred_element_type=...]
    unnamed x20 -> x15, local copies, waits for them, and re-layouts: 6.93 us -> 3.57 us
    all_gather x2 -> x0, local copies, waits for them, and re-layouts: 2.96 us -> none  [the longest x1 1.48 us: local(): value_all = lax.all_gather(values, 'col', axis=1, tiled=True)]
  transfers between devices with their start and end apart: 4 -> 3, of which waited for: 4 -> 3; matrix products, arithmetic and copies ran while one was open for 15% -> 10% of each run, Pallas kernels for 0% -> 0%
where the time goes in v3:
time: 173 us; the launch traced here: 172 us
  waiting for transfers between devices  103 us (60%)
  matrix products  17.2 us (10%)
  local copies, waits for them, and re-layouts  15.4 us (9%)
  between operations  14.2 us (8%)
  starting transfers between devices  13.9 us (8%)
  other arithmetic  8.26 us (5%)
    all_to_all x1, waiting for transfers between devices, local(): lax.all_to_all(bias_part.reshape(head_count, local_cols, row_count, row_k...  44.5 us
    all_gather x1, waiting for transfers between devices, local(): lax.all_gather(jnp.concatenate((keys, values), axis=2), 'col', axis=1, ti...  33.5 us
    all_to_all x1, waiting for transfers between devices, local(): lax.all_to_all(kv_part.reshape(slab_rows, col_count, local_cols, 2 * chan...  25.1 us
    all_to_all x1, starting transfers between devices, local(): lax.all_to_all(bias_part.reshape(head_count, local_cols, row_count, row_k...  8.85 us
    all_to_all x1, starting transfers between devices, local(): lax.all_to_all(kv_part.reshape(slab_rows, col_count, local_cols, 2 * chan...  4.97 us
    dot_general x1, matrix products, local(): jnp.einsum('rjhd,rkhd->rhjk', out_grad, value_heads, preferred_element_ty...  4.96 us
    dot_general x1, matrix products, local(): jnp.einsum('rjhd,rkhd->rhjk', query_heads, key_heads, preferred_element_t...  4.46 us
    convert_element_type x1, local copies, waits for them, and re-layouts, local(): scores = products * score_scale + bias.astype(jnp.float32)[None]  4.13 us
  transfers between devices with their start and end apart: 3, of which 3 were waited for; matrix products, arithmetic and copies ran while one was open for 10% of the time, Pallas kernels for 0%

profile of v3, /device:TPU:8, one launch (start us, length us, event | category | flops | bytes accessed | tf_op | source)
XLA Modules:
  0.0 172.1 jit_solution(1535113322949408808)
XLA Ops:
  7.2 0.0 copy-start
  7.2 0.0 copy-start.3
  7.2 0.0 all-gather.2.cloned.1.call-start
  7.2 1.5 pad_maximum_fusion.1
  8.8 0.0 all-gather.2.cloned.1.call-update
  8.8 0.9 copy.65
  9.8 0.9 add_divide_fusion
  10.6 0.1 copy.66
  10.7 4.1 %copy.64 = f32[4,128,2048]{1,2,0:T(8,128)} copy(bf16[4,128,2048]{2,1,0:T(8,128)(2,1)} %param.11) | data formatting | bytes 6291456 | tf_op jit(solution)/shard_map/convert_element_type | solution.py:36
  14.9 0.0 copy-done.3
  14.9 0.1 copy.63
  15.0 0.0 copy-done
  15.0 0.6 gather_fusion
  15.8 33.5 %all-gather.2.cloned.1.call-done = bf16[2,2048,256]{2,1,0:T(8,128)(2,1)} async-done(((bf16[2,128,256]{2,1,0:T(8,128)(2,1)}), bf16[2,2048,256]{2,1,0:T(8,128)(2,1)}) %all-gather.2.cloned.1.call-update) | async-done | bytes 2097168 | tf_op jit(solution)/shard_map/all_gather | solution.py:22
  49.3 1.7 fusion.15
  51.0 0.5 copy.61
  51.5 0.5 copy.67
  52.0 0.1 broadcast_in_dim.32
  52.1 4.5 %fusion.16 = (f32[2,4,128]{2,1,0:T(4,128)S(1)}, f32[2,4,128,2048]{2,3,1,0:T(8,128)S(1)}) fusion(f32[4,128,2048]{1,2,0:T(8,128)} %copy.64, bf16[2,2048,4,32]{1,3,2,0:T(8,128)(2,1)S(1)} %bitcast.49, bf16[2,128,4,32]{1,3,2,0:T(8,128)(2,1)S(1)} %bitcast.59, pred[128,2048]{0,1:T(8,128)(4,1)S(1)} %bitcast.58), kind=kOutput, calls=%fused_computation.42 | convolution fusion | flops 142605312 | bytes 13963264 | tf_op jit(solution)/shard_map/rjhd,rkhd->rhjk/dot_general | solution.py:33
  56.6 1.1 exponential_reduce_fusion
  57.7 1.7 %multiply_reduce_fusion = (f32[2,128,4]{1,2,0:T(4,128)S(1)}, bf16[2,128,4,32]{1,3,2,0:T(8,128)(2,1)S(1)}, bf16[2,128,4,32]{1,3,2,0:T(8,128)(2,1)S(1)}) fusion(f32[2,128,4,32]{1,3,2,0:T(8,128)S(1)} %bitcast.61, f32[2,128,4,32]{1,3,2,0:T(8,128)S(1)} %bitcast.62, bf16[2,2048,4,32]{1,3,2,0:T(8,128)(2,1)S(1)} %bitcast.51, ...), kind=kOutput, calls=%fused_computation.23 | convolution fusion | flops 138738688 | bytes 9838592 | tf_op jit(solution)/shard_map/rhjk,rkhd->rjhd/dot_general | solution.py:42
  59.5 1.5 convolution_convert_fusion
  61.0 5.0 %fusion.17 = (bf16[4,128,2048]{1,2,0:T(8,128)(2,1)}, bf16[2,4,128,2048]{2,3,1,0:T(8,128)(2,1)S(1)}) fusion(f32[2,4,128]{2,1,0:T(4,128)S(1)} %bitcast.70, bf16[2,128,4,32]{1,3,2,0:T(8,128)(2,1)S(1)} %get-tuple-element.26, bf16[2,2048,4,32]{1,3,2,0:T(8,128)(2,1)S(1)} %bitcast.52, f32[2,4,128,2048]{2,3,1,0:T(8,128)S(1)} %get-tuple-element.31, ...), kind=kOutput, calls=%fused_computation.43 | convolution fusion | flops 143654912 | bytes 15802368 | tf_op jit(solution)/shard_map/rjhd,rkhd->rhjk/dot_general | solution.py:56
  66.0 0.0 copy-start.1
  66.0 0.2 copy.88
  66.2 0.3 copy.74
  66.5 1.5 convolution_convert_fusion.1
  68.0 0.0 copy-done.1
  68.0 0.2 copy.87
  68.3 0.3 copy.73
  68.6 0.0 copy-start.2
  68.6 1.6 pad_maximum_fusion
  70.2 5.0 %all-to-all-start = ((bf16[2,16,128,256]{2,3,0,1:T(8,128)(2,1)}), bf16[2,16,128,256]{2,3,0,1:T(8,128)(2,1)}, u32[]{:S(2)}, u32[]{:S(2)}) async-start(bf16[2,16,128,256]{2,3,0,1:T(8,128)(2,1)} %pad_maximum_fusion), calls=%async_computation | async-start | bytes 4194304 | tf_op jit(solution)/shard_map/all_to_all | solution.py:74
  75.2 0.0 copy-done.2
  75.2 2.6 %copy.76 = bf16[4,128,16,128]{3,1,0,2:T(8,128)(2,1)} copy(bf16[4,128,16,128]{1,3,2,0:T(8,128)(2,1)S(1)} %bitcast.53) | data formatting | bytes 4194304 | tf_op jit(solution)/shard_map/convert_element_type | solution.py:71
  77.8 25.1 %all-to-all-done = bf16[2,16,128,256]{2,3,0,1:T(8,128)(2,1)} async-done(((bf16[2,16,128,256]{2,3,0,1:T(8,128)(2,1)}), bf16[2,16,128,256]{2,3,0,1:T(8,128)(2,1)}, u32[]{:S(2)}, u32[]{:S(2)}) %all-to-all-start) | async-done | bytes 2097184 | tf_op jit(solution)/shard_map/all_to_all | solution.py:74
  102.9 8.8 %all-to-all-start.1 = ((bf16[4,128,16,128]{3,1,0,2:T(8,128)(2,1)}), bf16[4,128,16,128]{3,1,0,2:T(8,128)(2,1)S(1)}, u32[]{:S(2)}, u32[]{:S(2)}) async-start(bf16[4,128,16,128]{3,1,0,2:T(8,128)(2,1)} %copy.76), calls=%async_computation.1 | async-start | bytes 4194304 | tf_op jit(solution)/shard_map/all_to_all | solution.py:82
  111.8 3.0 %fusion.8 = bf16[2,4,32,128]{3,2,1,0:T(8,128)(2,1)S(1)} fusion(bf16[2,2048,4,32]{1,3,2,0:T(8,128)(2,1)S(1)} %bitcast.50, bf16[2,4,128,2048]{2,3,1,0:T(8,128)(2,1)} %copy-done.1), kind=kOutput, calls=%fused_computation.17 | convolution fusion | flops 134283264 | bytes 5308416 | tf_op jit(solution)/shard_map/rhjk,rkhd->rjhd/dot_general | solution.py:61
  114.8 0.7 copy.77
  115.5 0.7 copy.80
  116.2 1.9 %convert_reduce_fusion.1 = f32[2,128,256]{1,2,0:T(8,128)S(1)} fusion(bf16[2,16,128,256]{2,3,0,1:T(8,128)(2,1)} %all-to-all-done), kind=kLoop, calls=%fused_computation.8 | loop fusion | flops 2031616 | bytes 2359296 | tf_op jit(solution)/shard_map/reduce_sum | solution.py:77
  118.2 0.7 copy.78
  118.9 0.7 copy.79
  119.7 44.5 %all-to-all-done.1 = bf16[4,128,16,128]{3,1,0,2:T(8,128)(2,1)S(1)} async-done(((bf16[4,128,16,128]{3,1,0,2:T(8,128)(2,1)}), bf16[4,128,16,128]{3,1,0,2:T(8,128)(2,1)S(1)}, u32[]{:S(2)}, u32[]{:S(2)}) %all-to-all-start.1) | async-done | bytes 2097184 | tf_op jit(solution)/shard_map/all_to_all | solution.py:82
  164.2 1.1 convert_reduce_fusion
  (8 shorter events, 0.1 us)
Async XLA Ops:
  7.2 7.9 %copy-start = (s32[16,16]{1,0:T(8,128)S(1)}, s32[16,16]{1,0:T(8,128)}, u32[]{:S(2)}) copy-start(s32[16,16]{1,0:T(8,128)} %param.13) | copy-start | bytes 3076
  7.2 7.7 %copy-start.3 = (bf16[2,128,128]{2,1,0:T(8,128)(2,1)S(1)}, bf16[2,128,128]{2,1,0:T(8,128)(2,1)}, u32[]{:S(2)}) copy-start(bf16[2,128,128]{2,1,0:T(8,128)(2,1)} %param.7) | copy-start | bytes 196612
  7.2 42.1 %all-gather.2.cloned.1.call-start = ((), (), s32[]{:S(2)}) async-start(), calls=%async_computation.2 | async-start | bytes 2228224 | tf_op jit(solution)/shard_map/all_gather | solution.py:22
  66.0 2.1 %copy-start.1 = (bf16[2,4,128,2048]{2,3,1,0:T(8,128)(2,1)}, bf16[2,4,128,2048]{2,3,1,0:T(8,128)(2,1)S(1)}, u32[]{:S(2)}) copy-start(bf16[2,4,128,2048]{2,3,1,0:T(8,128)(2,1)S(1)} %get-tuple-element.33) | copy-start | bytes 12582916
  68.6 6.6 %copy-start.2 = (bf16[4,128,2048]{1,2,0:T(8,128)(2,1)S(1)}, bf16[4,128,2048]{1,2,0:T(8,128)(2,1)}, u32[]{:S(2)}) copy-start(bf16[4,128,2048]{1,2,0:T(8,128)(2,1)} %get-tuple-element.32) | copy-start | bytes 6291460
  70.2 32.7 %all-to-all-start = ((bf16[2,16,128,256]{2,3,0,1:T(8,128)(2,1)}), bf16[2,16,128,256]{2,3,0,1:T(8,128)(2,1)}, u32[]{:S(2)}, u32[]{:S(2)}) async-start(bf16[2,16,128,256]{2,3,0,1:T(8,128)(2,1)} %pad_maximum_fusion), calls=%async_computation | async-start | bytes 4194304 | tf_op jit(solution)/shard_map/all_to_all | solution.py:74
  102.9 61.2 %all-to-all-start.1 = ((bf16[4,128,16,128]{3,1,0,2:T(8,128)(2,1)}), bf16[4,128,16,128]{3,1,0,2:T(8,128)(2,1)S(1)}, u32[]{:S(2)}, u32[]{:S(2)}) async-start(bf16[4,128,16,128]{3,1,0,2:T(8,128)(2,1)} %copy.76), calls=%async_computation.1 | async-start | bytes 4194304 | tf_op jit(solution)/shard_map/all_to_all | solution.py:82
Sparse Core Ops, SparseCore 0:
  10.4 38.8 all-gather.1
